TPU v7x, 32 devices: a whole 2x2x4 slice. The times are simulated.
32 devices in a mesh: day: 8 (over z, x), pt: 4 (over y, core).
Axes of the slice: x: 2, y: 2, z: 4, core: 2. Of those that a mesh axis runs over, the one named last changes fastest.
Arguments:
- points: bfloat16 [8, 64, 2048], P('day', None, 'pt'), may hold values from -0.45 to 0.45
- cells: bfloat16 [8, 64, 8192], P('day', None, 'pt'), may hold values from -0.44921875 to 0.44921875
- clone_weight: float32 [8, 64, 2048], P('day', None, 'pt'), may hold values from 0.1 to 1
- potential: float32 [8, 2048], P('day', 'pt'), may hold values from 0.2 to 5
- support_count: int32 [8], P('day'), may hold values from 512 to 2048, as said below
- cell_count: int32 [8], P('day'), may hold values from 2048 to 8192, as said below
Outputs:
- forward_message: float32 [8, 64, 2048], P('day', None, 'pt')
- backward_message: float32 [8, 64, 2048], P('day', None, 'pt')
- fit_ratio: float32 [8, 2048], P('day', 'pt')
Inputs may be any that keep to these rules, and one draw needn't show every extreme that they name: Live support points of a day are its first support_count slots; some day has all 2048 slots live and some day has 512. Observed cells of a day are its first cell_count slots; some day fills all 8192 slots and some day has 2048.
All inputs are finite; a program needn't handle non-finite values.
Results may differ from a plain program's by a relative error of at most 0.0003.
Values may be sent and summed in bfloat16 or wider, within the bound.
No kernel may reach another device: no remote copies, remote signals or barrier semaphores. Data moves between devices by JAX's collectives and lax.ppermute only.
A program may use at most 64 MiB of HBM per device.

v0:
```python
import jax
import jax.numpy as jnp
from jax import lax
from jax.sharding import PartitionSpec as P


def with_halo(cells, sides, width):
    for axis, dim in sides:
        count = lax.axis_size(axis)
        ends = count - 1
        head = lax.slice_in_dim(cells, 0, width, axis=dim)
        tail = lax.slice_in_dim(cells, cells.shape[dim] - width, cells.shape[dim], axis=dim)
        cells = jnp.concatenate(
            [
                lax.ppermute(tail, axis, [(i, (i + 1) % count) for i in range(ends)]),
                cells,
                lax.ppermute(head, axis, [((i + 1) % count, i) for i in range(ends)]),
            ],
            axis=dim,
        )
    return cells


def shifted(block, axis, distance):
    devices = range(lax.axis_size(axis))
    route = [(i - distance, i) for i in devices if i - distance in devices]
    return lax.ppermute(block, axis, route)


def norm_of(coords):
    wide = coords.astype(jnp.float32)
    return jnp.sum(wide * wide, axis=0)


def squared_dist(left_pts, left_norm, right_pts, right_norm):
    inner = lax.dot_general(
        left_pts, right_pts, (((0,), (0,)), ((), ())), preferred_element_type=jnp.float32
    )
    return left_norm[:, None] + right_norm[None, :] - 2.0 * inner


def shards(points, cells, clone_weight, potential, support_count, cell_count):
    pt_rank = lax.axis_index("pt")
    day_index = lax.axis_index("day")
    day_count = lax.axis_size("day")
    full_pts, full_clone, full_pot = (
        lax.all_gather(points.astype(jnp.float32), "pt", axis=2, tiled=True).astype(points.dtype),
        lax.all_gather(clone_weight, "pt", axis=2, tiled=True),
        lax.all_gather(potential, "pt", axis=1, tiled=True),
    )
    beside_all = with_halo(full_pts, (("day", 0),), 1)
    before_day = beside_all[0]
    after_day = beside_all[2]
    own_pts = points[0]
    per_device = own_pts.shape[1]
    support_total = full_pts.shape[2]
    clones = clone_weight.shape[1]
    weight = full_clone[0] * full_pot
    live_total = support_count[0].astype(jnp.float32)
    live_all = (jnp.arange(support_total, dtype=jnp.int32) < support_count[0]).astype(jnp.float32)
    live_own = lax.dynamic_slice_in_dim(live_all, pt_rank * per_device, per_device)
    own_norm = norm_of(own_pts)
    before_norm = norm_of(before_day)
    after_norm = norm_of(after_day)
    row_span = 512
    span_count = support_total // row_span

    def kernel_rows(source_pts, source_norm, block_index):
        offset = block_index * row_span
        source_rows = lax.dynamic_slice_in_dim(source_pts, offset, row_span, 1)
        norm_rows = lax.dynamic_slice_in_dim(source_norm, offset, row_span, 0)
        return jnp.exp(-squared_dist(source_rows, norm_rows, own_pts, own_norm)).astype(
            jnp.bfloat16
        )

    def contract(sent_rows, source_pts, source_norm):

        def add_rows(block_index, result):
            sent_part = lax.dynamic_slice_in_dim(sent_rows, block_index * row_span, row_span, 1)
            return result + jnp.dot(
                sent_part,
                kernel_rows(source_pts, source_norm, block_index),
                preferred_element_type=jnp.float32,
            )

        return lax.fori_loop(
            0, span_count, add_rows, jnp.zeros((sent_rows.shape[0], per_device), jnp.float32)
        )

    block_count = 4
    block_rows = clones // block_count
    steps_total = day_count + block_count - 1
    empty_rows = jnp.zeros((block_rows, per_device), jnp.float32)
    seed_rows = jnp.broadcast_to(live_own[None, :], (block_rows, per_device))

    def settle(piece_rows, full_rows, valid):
        column_sums = jnp.sum(full_rows * live_all[None, :], axis=1, keepdims=True)
        column_sums = jnp.where(valid, column_sums, 1.0)
        own_part = piece_rows * live_own[None, :] * live_total / column_sums
        whole_part = full_rows * live_all[None, :] * live_total / column_sums
        return (own_part, whole_part)

    def one_step(step_index, carried):
        forward_in, backward_in, forward_out, backward_out = carried
        forward_at = step_index - day_index
        forward_ok = (forward_at >= 0) & (forward_at < block_count)
        forward_block = jnp.clip(forward_at, 0, block_count - 1)
        backward_at = step_index - (day_count - 1 - day_index)
        backward_ok = (backward_at >= 0) & (backward_at < block_count)
        backward_block = jnp.clip(backward_at, 0, block_count - 1)
        forward_got = lax.cond(
            forward_ok & (day_index > 0),
            lambda: contract(forward_in, before_day, before_norm),
            lambda: empty_rows,
        )
        forward_piece = jnp.where(day_index == 0, seed_rows, forward_got)
        backward_got = lax.cond(
            backward_ok & (day_index < day_count - 1),
            lambda: contract(backward_in, after_day, after_norm),
            lambda: empty_rows,
        )
        backward_piece = jnp.where(day_index == day_count - 1, seed_rows, backward_got)
        forward_full, backward_full = (
            lax.all_gather(forward_piece, "pt", axis=1, tiled=True),
            lax.all_gather(backward_piece, "pt", axis=1, tiled=True),
        )
        forward_own, forward_all = settle(forward_piece, forward_full, forward_ok)
        backward_own, backward_all = settle(backward_piece, backward_full, backward_ok)
        forward_out = jnp.where(
            forward_ok,
            lax.dynamic_update_slice_in_dim(
                forward_out, forward_own, forward_block * block_rows, 0
            ),
            forward_out,
        )
        backward_out = jnp.where(
            backward_ok,
            lax.dynamic_update_slice_in_dim(
                backward_out, backward_own, backward_block * block_rows, 0
            ),
            backward_out,
        )
        forward_sent = (
            forward_all
            * lax.dynamic_slice_in_dim(weight, forward_block * block_rows, block_rows, 0)
        ).astype(jnp.bfloat16)
        backward_sent = (
            backward_all
            * lax.dynamic_slice_in_dim(weight, backward_block * block_rows, block_rows, 0)
        ).astype(jnp.bfloat16)
        forward_in = shifted(forward_sent, "day", 1)
        backward_in = shifted(backward_sent, "day", -1)
        return (forward_in, backward_in, forward_out, backward_out)

    start_in = jnp.zeros((block_rows, support_total), jnp.bfloat16)
    start_out = jnp.zeros((clones, per_device), jnp.float32)
    carried = lax.fori_loop(0, steps_total, one_step, (start_in, start_in, start_out, start_out))
    forward_out = carried[2]
    backward_out = carried[3]
    mass_own = (
        live_own * potential[0] * jnp.sum(forward_out * clone_weight[0] * backward_out, axis=0)
    )
    cell_total = cell_count[0]
    cell_total_f = cell_total.astype(jnp.float32)
    full_mass = lax.all_gather(mass_own, "pt", axis=0, tiled=True)
    mass_total = jnp.sum(full_mass)
    own_cells = cells[0]
    cell_norm = norm_of(own_cells)
    own_slots = own_cells.shape[1]
    day_pts = full_pts[0]
    day_norm = norm_of(day_pts)
    fit_span = 256
    fit_blocks = support_total // fit_span

    def fit_rows(block_index):
        offset = block_index * fit_span
        chosen = lax.dynamic_slice_in_dim(day_pts, offset, fit_span, 1)
        chosen_norm = lax.dynamic_slice_in_dim(day_norm, offset, fit_span, 0)
        return jnp.exp(-squared_dist(chosen, chosen_norm, own_cells, cell_norm))

    def density_part(block_index):
        chosen_mass = lax.dynamic_slice_in_dim(full_mass, block_index * fit_span, fit_span, 0)
        return jnp.dot(chosen_mass, fit_rows(block_index), precision=lax.Precision.HIGHEST)

    density = jnp.sum(lax.map(density_part, jnp.arange(fit_blocks)), axis=0) / mass_total
    cell_live = (pt_rank * own_slots + jnp.arange(own_slots, dtype=jnp.int32) < cell_total).astype(
        jnp.float32
    )
    inverse = cell_live / density

    def ratio_part(block_index):
        return jnp.dot(fit_rows(block_index), inverse, precision=lax.Precision.HIGHEST)

    ratio_rows = lax.map(ratio_part, jnp.arange(fit_blocks)).reshape(support_total)
    summed = lax.psum_scatter(ratio_rows, "pt", scatter_dimension=0, tiled=True)
    fit_rows_out = live_own / cell_total_f * summed
    return (forward_out[None], backward_out[None], fit_rows_out[None])


def solution(mesh):
    in_specs = (
        P("day", None, "pt"),
        P("day", None, "pt"),
        P("day", None, "pt"),
        P("day", "pt"),
        P("day"),
        P("day"),
    )
    out_specs = (P("day", None, "pt"), P("day", None, "pt"), P("day", "pt"))
    return jax.shard_map(shards, mesh=mesh, in_specs=in_specs, out_specs=out_specs, check_vma=False)
```

profile of v0, /device:TPU:0, one launch (start us, length us, event | category | flops | bytes accessed | tf_op | source)
XLA Modules:
  0.0 437.7 jit_solution(1554293441669828181)
XLA Ops:
  0.7 7.6 %all_gather.28 = bf16[1,64,2048]{2,1,0:T(8,128)(2,1)S(1)} all-gather(bf16[1,64,512]{2,1,0:T(8,128)(2,1)} %param.20), channel_id=1, replica_groups=mesh['day'=8,'pt'=4] {'pt'}, dimensions={2}, use_global_device_ids=true | all-gather | bytes 327680 | tf_op jit(solution)/shard_map/all_gather | solution.py:47
  14.2 7.4 %all_gather.29 = f32[1,64,2048]{2,1,0:T(8,128)S(1)} all-gather(f32[1,64,512]{2,1,0:T(8,128)} %param.22), channel_id=1, replica_groups=mesh['day'=8,'pt'=4] {'pt'}, dimensions={2}, use_global_device_ids=true | all-gather | bytes 655360 | tf_op jit(solution)/shard_map/all_gather | solution.py:48
  30.0 338.5 %while.72 = (s32[]{:T(128)}, bf16[16,2048]{1,0:T(8,128)(2,1)S(1)}, bf16[16,2048]{1,0:T(8,128)(2,1)S(1)}, f32[64,512]{1,0:T(8,128)S(1)}, f32[64,512]{1,0:T(8,128)...) while((s32[]{:T(128)}, bf16[16,2048]{1,0:T(8,128)(2,1)S(1)}, ...), condition=%wide.region_14.15_spmd.clone.clone, body=%wide.region_3.14_spmd.clone.clone.sunk | while | flops 87085088 | bytes 2573997 | solution.py:157
  56.2 5.4 %all_gather.38 = f32[16,2048]{1,0:T(8,128)S(1)} all-gather(f32[16,512]{1,0:T(8,128)S(1)} %get-tuple-element.1308), channel_id=1, replica_groups=mesh['day'=8,'pt'=4] {'pt'}, dimensions={1}, use_global_device_ids=true | all-gather | bytes 163840 | tf_op jit(solution)/shard_map/while/body/eval_jaxpr/all_gather | solution.py:125
  68.0 9.9 %collective-permute-start = (bf16[16,2048]{1,0:T(8,128)(2,1)S(1)}, bf16[16,2048]{1,0:T(8,128)(2,1)S(1)}, u32[]{:S(2)}, u32[]{:S(2)}) collective-permute-start(bf16[16,2048]{1,0:T(8,128)(2,1)S(1)} %get-tuple-element.1314), channel_id=1, source_target_pairs={{0,4},{4,8},{8,12},{12,16},{16,20},{20,24},{24,28},{1,5},{5,9},{9,... | collective-permute-start | bytes 196616 | tf_op jit(solution)/shard_map/while/body/eval_jaxpr/ppermute | solution.py:27
  97.8 9.3 %collective-permute-start = (bf16[16,2048]{1,0:T(8,128)(2,1)S(1)}, bf16[16,2048]{1,0:T(8,128)(2,1)S(1)}, u32[]{:S(2)}, u32[]{:S(2)}) collective-permute-start(bf16[16,2048]{1,0:T(8,128)(2,1)S(1)} %get-tuple-element.1314), channel_id=1, source_target_pairs={{0,4},{4,8},{8,12},{12,16},{16,20},{20,24},{24,28},{1,5},{5,9},{9,... | collective-permute-start | bytes 196616 | tf_op jit(solution)/shard_map/while/body/eval_jaxpr/ppermute | solution.py:27
  115.3 5.4 %all_gather.38 = f32[16,2048]{1,0:T(8,128)S(1)} all-gather(f32[16,512]{1,0:T(8,128)S(1)} %get-tuple-element.1308), channel_id=1, replica_groups=mesh['day'=8,'pt'=4] {'pt'}, dimensions={1}, use_global_device_ids=true | all-gather | bytes 163840 | tf_op jit(solution)/shard_map/while/body/eval_jaxpr/all_gather | solution.py:125
  127.0 9.3 %collective-permute-start = (bf16[16,2048]{1,0:T(8,128)(2,1)S(1)}, bf16[16,2048]{1,0:T(8,128)(2,1)S(1)}, u32[]{:S(2)}, u32[]{:S(2)}) collective-permute-start(bf16[16,2048]{1,0:T(8,128)(2,1)S(1)} %get-tuple-element.1314), channel_id=1, source_target_pairs={{0,4},{4,8},{8,12},{12,16},{16,20},{20,24},{24,28},{1,5},{5,9},{9,... | collective-permute-start | bytes 196616 | tf_op jit(solution)/shard_map/while/body/eval_jaxpr/ppermute | solution.py:27
  156.3 9.3 %collective-permute-start = (bf16[16,2048]{1,0:T(8,128)(2,1)S(1)}, bf16[16,2048]{1,0:T(8,128)(2,1)S(1)}, u32[]{:S(2)}, u32[]{:S(2)}) collective-permute-start(bf16[16,2048]{1,0:T(8,128)(2,1)S(1)} %get-tuple-element.1314), channel_id=1, source_target_pairs={{0,4},{4,8},{8,12},{12,16},{16,20},{20,24},{24,28},{1,5},{5,9},{9,... | collective-permute-start | bytes 196616 | tf_op jit(solution)/shard_map/while/body/eval_jaxpr/ppermute | solution.py:27
  185.5 11.0 %collective-permute-start = (bf16[16,2048]{1,0:T(8,128)(2,1)S(1)}, bf16[16,2048]{1,0:T(8,128)(2,1)S(1)}, u32[]{:S(2)}, u32[]{:S(2)}) collective-permute-start(bf16[16,2048]{1,0:T(8,128)(2,1)S(1)} %get-tuple-element.1314), channel_id=1, source_target_pairs={{0,4},{4,8},{8,12},{12,16},{16,20},{20,24},{24,28},{1,5},{5,9},{9,... | collective-permute-start | bytes 196616 | tf_op jit(solution)/shard_map/while/body/eval_jaxpr/ppermute | solution.py:27
  198.4 17.1 %collective-permute-done.1 = bf16[16,2048]{1,0:T(8,128)(2,1)S(1)} collective-permute-done((bf16[16,2048]{1,0:T(8,128)(2,1)S(1)}, bf16[16,2048]{1,0:T(8,128)(2,1)S(1)}, u32[]{:S(2)}, u32[]{:S(2)}) %collective-permute-start.1) | collective-permute-done | bytes 65568 | tf_op jit(solution)/shard_map/while/body/eval_jaxpr/ppermute | solution.py:27
  229.3 11.2 %collective-permute-start = (bf16[16,2048]{1,0:T(8,128)(2,1)S(1)}, bf16[16,2048]{1,0:T(8,128)(2,1)S(1)}, u32[]{:S(2)}, u32[]{:S(2)}) collective-permute-start(bf16[16,2048]{1,0:T(8,128)(2,1)S(1)} %get-tuple-element.1314), channel_id=1, source_target_pairs={{0,4},{4,8},{8,12},{12,16},{16,20},{20,24},{24,28},{1,5},{5,9},{9,... | collective-permute-start | bytes 196616 | tf_op jit(solution)/shard_map/while/body/eval_jaxpr/ppermute | solution.py:27
  246.6 7.0 %conditional.8 = (f32[16,512]{1,0:T(8,128)}) conditional(s32[]{:T(128)} %convert_element_type.133, () %tuple.157, (bf16[16,2048]{1,0:T(8,128)(2,1)S(1)}, f32[2048]{0:T(1024)S(1)}, f32[512]{0:T(512)S(1)}, bf16[64,2048]{1,0:T(8,128)(2,1)S(1)}, bf16[64,512]{1,0:T(8,128)(2,1)S(1)}) %tuple.158), branch_computations={%region_9.9_spmd, %region_10.12_spmd} | conditional | flops 43270152 | bytes 222992 | solution.py:117
  246.6 7.0 %while.69 = (s32[]{:T(128)}, f32[16,512]{1,0:T(8,128)}, bf16[16,2048]{1,0:T(8,128)(2,1)S(1)}, f32[2048]{0:T(1024)S(1)}, f32[512]{0:T(512)S(1)}, /*index=5*/bf16[...) while((s32[]{:T(128)}, f32[16,512]{1,0:T(8,128)}, ...), condition=%wide.region_12.11_spmd.clone, body=%wide.region_11.10_spmd.clone.sunk | while | flops 43270152 | bytes 222888 | solution.py:86
  266.8 7.5 %collective-permute-start = (bf16[16,2048]{1,0:T(8,128)(2,1)S(1)}, bf16[16,2048]{1,0:T(8,128)(2,1)S(1)}, u32[]{:S(2)}, u32[]{:S(2)}) collective-permute-start(bf16[16,2048]{1,0:T(8,128)(2,1)S(1)} %get-tuple-element.1314), channel_id=1, source_target_pairs={{0,4},{4,8},{8,12},{12,16},{16,20},{20,24},{24,28},{1,5},{5,9},{9,... | collective-permute-start | bytes 196616 | tf_op jit(solution)/shard_map/while/body/eval_jaxpr/ppermute | solution.py:27
  280.5 7.0 %conditional.8 = (f32[16,512]{1,0:T(8,128)}) conditional(s32[]{:T(128)} %convert_element_type.133, () %tuple.157, (bf16[16,2048]{1,0:T(8,128)(2,1)S(1)}, f32[2048]{0:T(1024)S(1)}, f32[512]{0:T(512)S(1)}, bf16[64,2048]{1,0:T(8,128)(2,1)S(1)}, bf16[64,512]{1,0:T(8,128)(2,1)S(1)}) %tuple.158), branch_computations={%region_9.9_spmd, %region_10.12_spmd} | conditional | flops 43270152 | bytes 222992 | solution.py:117
  280.5 7.0 %while.69 = (s32[]{:T(128)}, f32[16,512]{1,0:T(8,128)}, bf16[16,2048]{1,0:T(8,128)(2,1)S(1)}, f32[2048]{0:T(1024)S(1)}, f32[512]{0:T(512)S(1)}, /*index=5*/bf16[...) while((s32[]{:T(128)}, f32[16,512]{1,0:T(8,128)}, ...), condition=%wide.region_12.11_spmd.clone, body=%wide.region_11.10_spmd.clone.sunk | while | flops 43270152 | bytes 222888 | solution.py:86
  311.6 7.0 %conditional.8 = (f32[16,512]{1,0:T(8,128)}) conditional(s32[]{:T(128)} %convert_element_type.133, () %tuple.157, (bf16[16,2048]{1,0:T(8,128)(2,1)S(1)}, f32[2048]{0:T(1024)S(1)}, f32[512]{0:T(512)S(1)}, bf16[64,2048]{1,0:T(8,128)(2,1)S(1)}, bf16[64,512]{1,0:T(8,128)(2,1)S(1)}) %tuple.158), branch_computations={%region_9.9_spmd, %region_10.12_spmd} | conditional | flops 43270152 | bytes 222992 | solution.py:117
  311.6 7.0 %while.69 = (s32[]{:T(128)}, f32[16,512]{1,0:T(8,128)}, bf16[16,2048]{1,0:T(8,128)(2,1)S(1)}, f32[2048]{0:T(1024)S(1)}, f32[512]{0:T(512)S(1)}, /*index=5*/bf16[...) while((s32[]{:T(128)}, f32[16,512]{1,0:T(8,128)}, ...), condition=%wide.region_12.11_spmd.clone, body=%wide.region_11.10_spmd.clone.sunk | while | flops 43270152 | bytes 222888 | solution.py:86
  340.8 7.0 %conditional.8 = (f32[16,512]{1,0:T(8,128)}) conditional(s32[]{:T(128)} %convert_element_type.133, () %tuple.157, (bf16[16,2048]{1,0:T(8,128)(2,1)S(1)}, f32[2048]{0:T(1024)S(1)}, f32[512]{0:T(512)S(1)}, bf16[64,2048]{1,0:T(8,128)(2,1)S(1)}, bf16[64,512]{1,0:T(8,128)(2,1)S(1)}) %tuple.158), branch_computations={%region_9.9_spmd, %region_10.12_spmd} | conditional | flops 43270152 | bytes 222992 | solution.py:117
  340.8 7.0 %while.69 = (s32[]{:T(128)}, f32[16,512]{1,0:T(8,128)}, bf16[16,2048]{1,0:T(8,128)(2,1)S(1)}, f32[2048]{0:T(1024)S(1)}, f32[512]{0:T(512)S(1)}, /*index=5*/bf16[...) while((s32[]{:T(128)}, f32[16,512]{1,0:T(8,128)}, ...), condition=%wide.region_12.11_spmd.clone, body=%wide.region_11.10_spmd.clone.sunk | while | flops 43270152 | bytes 222888 | solution.py:86
  373.8 25.9 %while.70 = (s32[]{:T(128)}, f32[8,2048]{1,0:T(8,128)S(1)}, s32[8]{0:T(128)S(1)}, f32[2048]{0:T(1024)S(1)}, f32[2048]{0:T(1024)S(1)}, /*index=5*/f32[2048]{0:T(1...) while((s32[]{:T(128)}, f32[8,2048]{1,0:T(8,128)S(1)}, ...), condition=%wide.region_20.21_spmd, body=%wide.region_19.20_spmd.sunk | while | flops 75497480 | bytes 4528319 | solution.py:185
  401.0 29.2 %while.71 = (s32[]{:T(128)}, f32[8,256]{1,0:T(8,128)S(1)}, s32[8]{0:T(128)S(1)}, f32[2048]{0:T(1024)S(1)}, f32[2048]{0:T(1024)S(1)}, /*index=5*/bf16[64,2048]{1,...) while((s32[]{:T(128)}, f32[8,256]{1,0:T(8,128)S(1)}, ...), condition=%wide.region_23.24_spmd, body=%wide.region_22.23_spmd.sunk | while | flops 75497480 | bytes 4511931 | solution.py:194
  430.2 6.8 %all-reduce = f32[2048]{0:T(1024)S(1)} all-reduce(f32[2048]{0:T(1024)S(1)} %bitcast.86), channel_id=2, replica_groups=mesh['day'=8,'pt'=4] {'pt'}, use_global_device_ids=true, to_apply=%region_24.25.clone | all-reduce | flops 2048 | bytes 16384
  (325 shorter events, 317.0 us)
Async XLA Ops:
  8.3 21.4 %collective-permute-start.3 = (bf16[1,64,2048]{2,1,0:T(8,128)(2,1)S(1)}, bf16[1,64,2048]{2,1,0:T(8,128)(2,1)S(1)}, u32[]{:S(2)}, u32[]{:S(2)}) collective-permute-start(bf16[1,64,2048]{2,1,0:T(8,128)(2,1)S(1)} %all_gather.28), channel_id=1, source_target_pairs={{4,0},{8,4},{12,8},{16,12},{20,16},{24,20},{28,24},{5,1},{9,5},{13... | collective-permute-start | bytes 786440 | tf_op jit(solution)/shard_map/ppermute | solution.py:17
  9.5 20.2 %collective-permute-start.2 = (bf16[1,64,2048]{2,1,0:T(8,128)(2,1)S(1)}, bf16[1,64,2048]{2,1,0:T(8,128)(2,1)S(1)}, u32[]{:S(2)}, u32[]{:S(2)}) collective-permute-start(bf16[1,64,2048]{2,1,0:T(8,128)(2,1)S(1)} %all_gather.28), channel_id=1, source_target_pairs={{0,4},{4,8},{8,12},{12,16},{16,20},{20,24},{24,28},{1,5},{5,9},{9,... | collective-permute-start | bytes 786440 | tf_op jit(solution)/shard_map/ppermute | solution.py:15
  43.8 6.2 %collective-permute-start = (bf16[16,2048]{1,0:T(8,128)(2,1)S(1)}, bf16[16,2048]{1,0:T(8,128)(2,1)S(1)}, u32[]{:S(2)}, u32[]{:S(2)}) collective-permute-start(bf16[16,2048]{1,0:T(8,128)(2,1)S(1)} %get-tuple-element.1314), channel_id=1, source_target_pairs={{0,4},{4,8},{8,12},{12,16},{16,20},{20,24},{24,28},{1,5},{5,9},{9,... | collective-permute-start | bytes 196616 | tf_op jit(solution)/shard_map/while/body/eval_jaxpr/ppermute | solution.py:27
  48.1 6.2 %collective-permute-start.1 = (bf16[16,2048]{1,0:T(8,128)(2,1)S(1)}, bf16[16,2048]{1,0:T(8,128)(2,1)S(1)}, u32[]{:S(2)}, u32[]{:S(2)}) collective-permute-start(bf16[16,2048]{1,0:T(8,128)(2,1)S(1)} %get-tuple-element.1315), channel_id=1, source_target_pairs={{4,0},{8,4},{12,8},{16,12},{20,16},{24,20},{28,24},{5,1},{9,5},{13... | collective-permute-start | bytes 196616 | tf_op jit(solution)/shard_map/while/body/eval_jaxpr/ppermute | solution.py:27
  68.0 11.8 %collective-permute-start = (bf16[16,2048]{1,0:T(8,128)(2,1)S(1)}, bf16[16,2048]{1,0:T(8,128)(2,1)S(1)}, u32[]{:S(2)}, u32[]{:S(2)}) collective-permute-start(bf16[16,2048]{1,0:T(8,128)(2,1)S(1)} %get-tuple-element.1314), channel_id=1, source_target_pairs={{0,4},{4,8},{8,12},{12,16},{16,20},{20,24},{24,28},{1,5},{5,9},{9,... | collective-permute-start | bytes 196616 | tf_op jit(solution)/shard_map/while/body/eval_jaxpr/ppermute | solution.py:27
  77.9 6.2 %collective-permute-start.1 = (bf16[16,2048]{1,0:T(8,128)(2,1)S(1)}, bf16[16,2048]{1,0:T(8,128)(2,1)S(1)}, u32[]{:S(2)}, u32[]{:S(2)}) collective-permute-start(bf16[16,2048]{1,0:T(8,128)(2,1)S(1)} %get-tuple-element.1315), channel_id=1, source_target_pairs={{4,0},{8,4},{12,8},{16,12},{20,16},{24,20},{28,24},{5,1},{9,5},{13... | collective-permute-start | bytes 196616 | tf_op jit(solution)/shard_map/while/body/eval_jaxpr/ppermute | solution.py:27
  97.8 11.2 %collective-permute-start = (bf16[16,2048]{1,0:T(8,128)(2,1)S(1)}, bf16[16,2048]{1,0:T(8,128)(2,1)S(1)}, u32[]{:S(2)}, u32[]{:S(2)}) collective-permute-start(bf16[16,2048]{1,0:T(8,128)(2,1)S(1)} %get-tuple-element.1314), channel_id=1, source_target_pairs={{0,4},{4,8},{8,12},{12,16},{16,20},{20,24},{24,28},{1,5},{5,9},{9,... | collective-permute-start | bytes 196616 | tf_op jit(solution)/shard_map/while/body/eval_jaxpr/ppermute | solution.py:27
  107.1 6.2 %collective-permute-start.1 = (bf16[16,2048]{1,0:T(8,128)(2,1)S(1)}, bf16[16,2048]{1,0:T(8,128)(2,1)S(1)}, u32[]{:S(2)}, u32[]{:S(2)}) collective-permute-start(bf16[16,2048]{1,0:T(8,128)(2,1)S(1)} %get-tuple-element.1315), channel_id=1, source_target_pairs={{4,0},{8,4},{12,8},{16,12},{20,16},{24,20},{28,24},{5,1},{9,5},{13... | collective-permute-start | bytes 196616 | tf_op jit(solution)/shard_map/while/body/eval_jaxpr/ppermute | solution.py:27
  127.0 11.2 %collective-permute-start = (bf16[16,2048]{1,0:T(8,128)(2,1)S(1)}, bf16[16,2048]{1,0:T(8,128)(2,1)S(1)}, u32[]{:S(2)}, u32[]{:S(2)}) collective-permute-start(bf16[16,2048]{1,0:T(8,128)(2,1)S(1)} %get-tuple-element.1314), channel_id=1, source_target_pairs={{0,4},{4,8},{8,12},{12,16},{16,20},{20,24},{24,28},{1,5},{5,9},{9,... | collective-permute-start | bytes 196616 | tf_op jit(solution)/shard_map/while/body/eval_jaxpr/ppermute | solution.py:27
  136.4 6.2 %collective-permute-start.1 = (bf16[16,2048]{1,0:T(8,128)(2,1)S(1)}, bf16[16,2048]{1,0:T(8,128)(2,1)S(1)}, u32[]{:S(2)}, u32[]{:S(2)}) collective-permute-start(bf16[16,2048]{1,0:T(8,128)(2,1)S(1)} %get-tuple-element.1315), channel_id=1, source_target_pairs={{4,0},{8,4},{12,8},{16,12},{20,16},{24,20},{28,24},{5,1},{9,5},{13... | collective-permute-start | bytes 196616 | tf_op jit(solution)/shard_map/while/body/eval_jaxpr/ppermute | solution.py:27
  156.3 11.2 %collective-permute-start = (bf16[16,2048]{1,0:T(8,128)(2,1)S(1)}, bf16[16,2048]{1,0:T(8,128)(2,1)S(1)}, u32[]{:S(2)}, u32[]{:S(2)}) collective-permute-start(bf16[16,2048]{1,0:T(8,128)(2,1)S(1)} %get-tuple-element.1314), channel_id=1, source_target_pairs={{0,4},{4,8},{8,12},{12,16},{16,20},{20,24},{24,28},{1,5},{5,9},{9,... | collective-permute-start | bytes 196616 | tf_op jit(solution)/shard_map/while/body/eval_jaxpr/ppermute | solution.py:27
  165.6 6.2 %collective-permute-start.1 = (bf16[16,2048]{1,0:T(8,128)(2,1)S(1)}, bf16[16,2048]{1,0:T(8,128)(2,1)S(1)}, u32[]{:S(2)}, u32[]{:S(2)}) collective-permute-start(bf16[16,2048]{1,0:T(8,128)(2,1)S(1)} %get-tuple-element.1315), channel_id=1, source_target_pairs={{4,0},{8,4},{12,8},{16,12},{20,16},{24,20},{28,24},{5,1},{9,5},{13... | collective-permute-start | bytes 196616 | tf_op jit(solution)/shard_map/while/body/eval_jaxpr/ppermute | solution.py:27
  185.5 12.9 %collective-permute-start = (bf16[16,2048]{1,0:T(8,128)(2,1)S(1)}, bf16[16,2048]{1,0:T(8,128)(2,1)S(1)}, u32[]{:S(2)}, u32[]{:S(2)}) collective-permute-start(bf16[16,2048]{1,0:T(8,128)(2,1)S(1)} %get-tuple-element.1314), channel_id=1, source_target_pairs={{0,4},{4,8},{8,12},{12,16},{16,20},{20,24},{24,28},{1,5},{5,9},{9,... | collective-permute-start | bytes 196616 | tf_op jit(solution)/shard_map/while/body/eval_jaxpr/ppermute | solution.py:27
  196.5 19.0 %collective-permute-start.1 = (bf16[16,2048]{1,0:T(8,128)(2,1)S(1)}, bf16[16,2048]{1,0:T(8,128)(2,1)S(1)}, u32[]{:S(2)}, u32[]{:S(2)}) collective-permute-start(bf16[16,2048]{1,0:T(8,128)(2,1)S(1)} %get-tuple-element.1315), channel_id=1, source_target_pairs={{4,0},{8,4},{12,8},{16,12},{20,16},{24,20},{28,24},{5,1},{9,5},{13... | collective-permute-start | bytes 196616 | tf_op jit(solution)/shard_map/while/body/eval_jaxpr/ppermute | solution.py:27
  229.3 13.1 %collective-permute-start = (bf16[16,2048]{1,0:T(8,128)(2,1)S(1)}, bf16[16,2048]{1,0:T(8,128)(2,1)S(1)}, u32[]{:S(2)}, u32[]{:S(2)}) collective-permute-start(bf16[16,2048]{1,0:T(8,128)(2,1)S(1)} %get-tuple-element.1314), channel_id=1, source_target_pairs={{0,4},{4,8},{8,12},{12,16},{16,20},{20,24},{24,28},{1,5},{5,9},{9,... | collective-permute-start | bytes 196616 | tf_op jit(solution)/shard_map/while/body/eval_jaxpr/ppermute | solution.py:27
  240.5 6.2 %collective-permute-start.1 = (bf16[16,2048]{1,0:T(8,128)(2,1)S(1)}, bf16[16,2048]{1,0:T(8,128)(2,1)S(1)}, u32[]{:S(2)}, u32[]{:S(2)}) collective-permute-start(bf16[16,2048]{1,0:T(8,128)(2,1)S(1)} %get-tuple-element.1315), channel_id=1, source_target_pairs={{4,0},{8,4},{12,8},{16,12},{20,16},{24,20},{28,24},{5,1},{9,5},{13... | collective-permute-start | bytes 196616 | tf_op jit(solution)/shard_map/while/body/eval_jaxpr/ppermute | solution.py:27
  266.8 9.4 %collective-permute-start = (bf16[16,2048]{1,0:T(8,128)(2,1)S(1)}, bf16[16,2048]{1,0:T(8,128)(2,1)S(1)}, u32[]{:S(2)}, u32[]{:S(2)}) collective-permute-start(bf16[16,2048]{1,0:T(8,128)(2,1)S(1)} %get-tuple-element.1314), channel_id=1, source_target_pairs={{0,4},{4,8},{8,12},{12,16},{16,20},{20,24},{24,28},{1,5},{5,9},{9,... | collective-permute-start | bytes 196616 | tf_op jit(solution)/shard_map/while/body/eval_jaxpr/ppermute | solution.py:27
  274.3 6.2 %collective-permute-start.1 = (bf16[16,2048]{1,0:T(8,128)(2,1)S(1)}, bf16[16,2048]{1,0:T(8,128)(2,1)S(1)}, u32[]{:S(2)}, u32[]{:S(2)}) collective-permute-start(bf16[16,2048]{1,0:T(8,128)(2,1)S(1)} %get-tuple-element.1315), channel_id=1, source_target_pairs={{4,0},{8,4},{12,8},{16,12},{20,16},{24,20},{28,24},{5,1},{9,5},{13... | collective-permute-start | bytes 196616 | tf_op jit(solution)/shard_map/while/body/eval_jaxpr/ppermute | solution.py:27
  300.6 6.6 %collective-permute-start = (bf16[16,2048]{1,0:T(8,128)(2,1)S(1)}, bf16[16,2048]{1,0:T(8,128)(2,1)S(1)}, u32[]{:S(2)}, u32[]{:S(2)}) collective-permute-start(bf16[16,2048]{1,0:T(8,128)(2,1)S(1)} %get-tuple-element.1314), channel_id=1, source_target_pairs={{0,4},{4,8},{8,12},{12,16},{16,20},{20,24},{24,28},{1,5},{5,9},{9,... | collective-permute-start | bytes 196616 | tf_op jit(solution)/shard_map/while/body/eval_jaxpr/ppermute | solution.py:27
  305.4 6.2 %collective-permute-start.1 = (bf16[16,2048]{1,0:T(8,128)(2,1)S(1)}, bf16[16,2048]{1,0:T(8,128)(2,1)S(1)}, u32[]{:S(2)}, u32[]{:S(2)}) collective-permute-start(bf16[16,2048]{1,0:T(8,128)(2,1)S(1)} %get-tuple-element.1315), channel_id=1, source_target_pairs={{4,0},{8,4},{12,8},{16,12},{20,16},{24,20},{28,24},{5,1},{9,5},{13... | collective-permute-start | bytes 196616 | tf_op jit(solution)/shard_map/while/body/eval_jaxpr/ppermute | solution.py:27
  331.7 4.8 %collective-permute-start = (bf16[16,2048]{1,0:T(8,128)(2,1)S(1)}, bf16[16,2048]{1,0:T(8,128)(2,1)S(1)}, u32[]{:S(2)}, u32[]{:S(2)}) collective-permute-start(bf16[16,2048]{1,0:T(8,128)(2,1)S(1)} %get-tuple-element.1314), channel_id=1, source_target_pairs={{0,4},{4,8},{8,12},{12,16},{16,20},{20,24},{24,28},{1,5},{5,9},{9,... | collective-permute-start | bytes 196616 | tf_op jit(solution)/shard_map/while/body/eval_jaxpr/ppermute | solution.py:27
  334.6 6.2 %collective-permute-start.1 = (bf16[16,2048]{1,0:T(8,128)(2,1)S(1)}, bf16[16,2048]{1,0:T(8,128)(2,1)S(1)}, u32[]{:S(2)}, u32[]{:S(2)}) collective-permute-start(bf16[16,2048]{1,0:T(8,128)(2,1)S(1)} %get-tuple-element.1315), channel_id=1, source_target_pairs={{4,0},{8,4},{12,8},{16,12},{20,16},{24,20},{28,24},{5,1},{9,5},{13... | collective-permute-start | bytes 196616 | tf_op jit(solution)/shard_map/while/body/eval_jaxpr/ppermute | solution.py:27
  361.0 3.4 collective-permute-start
  362.3 6.2 %collective-permute-start.1 = (bf16[16,2048]{1,0:T(8,128)(2,1)S(1)}, bf16[16,2048]{1,0:T(8,128)(2,1)S(1)}, u32[]{:S(2)}, u32[]{:S(2)}) collective-permute-start(bf16[16,2048]{1,0:T(8,128)(2,1)S(1)} %get-tuple-element.1315), channel_id=1, source_target_pairs={{4,0},{8,4},{12,8},{16,12},{20,16},{24,20},{28,24},{5,1},{9,5},{13... | collective-permute-start | bytes 196616 | tf_op jit(solution)/shard_map/while/body/eval_jaxpr/ppermute | solution.py:27
  (7 other events, 770.8 us)
where the time goes:
time: 441 us; the launch traced here: 438 us
  blocking collectives  151 us (34%)
  starting transfers between devices  101 us (23%)
  waiting for transfers between devices  65.4 us (15%)
  matrix products  58.2 us (13%)
  local copies, waits for them, and re-layouts  25.9 us (6%)
  other arithmetic  21.6 us (5%)
  loops' own time  11.7 us (3%)
    ppermute x22, starting transfers between devices, shifted(): return lax.ppermute(block, axis, route)  95 us
    ppermute x22, waiting for transfers between devices, shifted(): return lax.ppermute(block, axis, route)  65.4 us
    all_gather x11, blocking collectives, one_step(): lax.all_gather(backward_piece, 'pt', axis=1, tiled=True)  59.5 us
    all_gather x11, blocking collectives, one_step(): lax.all_gather(forward_piece, 'pt', axis=1, tiled=True)  59.4 us
    dot_general x16, matrix products, add_rows(): jnp.dot(sent_part, kernel_rows(source_pts, source_norm, block_index), pre...  27 us
    dot_general x8, matrix products, ratio_part(): jnp.dot(fit_rows(block_index), inverse, precision=lax.Precision.HIGHEST)  13.8 us
    another operation x18, local copies, waits for them, and re-layouts  11.1 us
    dynamic_slice x16, local copies, waits for them, and re-layouts, shards(): lax.map(density_part, jnp.arange(fit_blocks))  9.38 us
  transfers between devices with their start and end apart: 24, of which 22 were waited for; matrix products, arithmetic and copies ran while one was open for 0% of the time, Pallas kernels for 0%

commit v1 on v0

--- a/solution.py
+++ b/solution.py
@@ -2,6 +2,19 @@
 import jax.numpy as jnp
 from jax import lax
 from jax.sharding import PartitionSpec as P
+
+
+def collect(array, axis, dim):
+    ways = lax.axis_size(axis)
+    up = [(d, (d + 1) % ways) for d in range(ways)]
+    down = [(d, (d - 1) % ways) for d in range(ways)]
+    earlier, later = ([array], [array])
+    for _ in range(ways // 2):
+        earlier.append(lax.ppermute(earlier[-1], axis, up))
+    for _ in range((ways - 1) // 2):
+        later.append(lax.ppermute(later[-1], axis, down))
+    line = jnp.concatenate([*earlier[::-1], *later[1:]], axis=dim)
+    return jnp.roll(line, (lax.axis_index(axis) - ways // 2) * array.shape[dim], axis=dim)
 
 
 def with_halo(cells, sides, width):
@@ -122,7 +135,7 @@
         backward_piece = jnp.where(day_index == day_count - 1, seed_rows, backward_got)
         forward_full, backward_full = (
             lax.all_gather(forward_piece, "pt", axis=1, tiled=True),
-            lax.all_gather(backward_piece, "pt", axis=1, tiled=True),
+            collect(backward_piece, "pt", 1),
         )
         forward_own, forward_all = settle(forward_piece, forward_full, forward_ok)
         backward_own, backward_all = settle(backward_piece, backward_full, backward_ok)

time: 441 us -> 415 us (0.941)
  blocking collectives: 151 us -> 94.1 us
  starting transfers between devices: 101 us -> 121 us
  waiting for transfers between devices: 65.4 us -> 75.2 us
    all_gather x11 -> x0, blocking collectives: 59.5 us -> none  [one_step(): lax.all_gather(backward_piece, 'pt', axis=1, tiled=True)]
    ppermute x0 -> x33, starting transfers between devices: none -> 19.7 us  [the longest x11 18.7 us: collect(): later.append(lax.ppermute(later[-1], axis, down))]
    ppermute x0 -> x33, waiting for transfers between devices: none -> 9.84 us  [the longest x22 9.81 us: collect(): earlier.append(lax.ppermute(earlier[-1], axis, up))]
  transfers between devices with their start and end apart: 24 -> 57, of which waited for: 22 -> 33; matrix products, arithmetic and copies ran while one was open for 0% -> 2% of each run, Pallas kernels for 0% -> 0%
where the time goes in v1:
time: 415 us; the launch traced here: 412 us
  starting transfers between devices  121 us (29%)
  blocking collectives  94.1 us (23%)
  waiting for transfers between devices  75.2 us (18%)
  matrix products  58.2 us (14%)
  local copies, waits for them, and re-layouts  26.3 us (6%)
  other arithmetic  21.7 us (5%)
  loops' own time  12.8 us (3%)
    ppermute x22, starting transfers between devices, shifted(): return lax.ppermute(block, axis, route)  95 us
    ppermute x22, waiting for transfers between devices, shifted(): return lax.ppermute(block, axis, route)  65.4 us
    all_gather x11, blocking collectives, one_step(): lax.all_gather(forward_piece, 'pt', axis=1, tiled=True)  61.4 us
    dot_general x16, matrix products, add_rows(): jnp.dot(sent_part, kernel_rows(source_pts, source_norm, block_index), pre...  27 us
    ppermute x11, starting transfers between devices, collect(): later.append(lax.ppermute(later[-1], axis, down))  18.7 us
    dot_general x8, matrix products, ratio_part(): jnp.dot(fit_rows(block_index), inverse, precision=lax.Precision.HIGHEST)  13.8 us
    another operation x18, local copies, waits for them, and re-layouts  11.1 us
    ppermute x22, waiting for transfers between devices, collect(): earlier.append(lax.ppermute(earlier[-1], axis, up))  9.81 us
  transfers between devices with their start and end apart: 57, of which 33 were waited for; matrix products, arithmetic and copies ran while one was open for 2% of the time, Pallas kernels for 0%

profile of v1, /device:TPU:0, one launch (start us, length us, event | category | flops | bytes accessed | tf_op | source)
XLA Modules:
  0.0 411.7 jit_solution(5748715314064413350)
XLA Ops:
  0.7 7.6 %all_gather.22 = bf16[1,64,2048]{2,1,0:T(8,128)(2,1)S(1)} all-gather(bf16[1,64,512]{2,1,0:T(8,128)(2,1)} %param.20), channel_id=1, replica_groups=mesh['day'=8,'pt'=4] {'pt'}, dimensions={2}, use_global_device_ids=true | all-gather | bytes 327680 | tf_op jit(solution)/shard_map/all_gather | solution.py:60
  14.2 7.4 %all_gather.23 = f32[1,64,2048]{2,1,0:T(8,128)S(1)} all-gather(f32[1,64,512]{2,1,0:T(8,128)} %param.22), channel_id=1, replica_groups=mesh['day'=8,'pt'=4] {'pt'}, dimensions={2}, use_global_device_ids=true | all-gather | bytes 655360 | tf_op jit(solution)/shard_map/all_gather | solution.py:61
  30.0 312.2 %while.73 = (s32[]{:T(128)}, bf16[16,2048]{1,0:T(8,128)(2,1)S(1)}, bf16[16,2048]{1,0:T(8,128)(2,1)S(1)}, f32[64,512]{1,0:T(8,128)S(1)}, f32[64,512]{1,0:T(8,128)...) while((s32[]{:T(128)}, bf16[16,2048]{1,0:T(8,128)(2,1)S(1)}, ...), condition=%wide.region_14.15_spmd.clone.clone, body=%wide.region_3.14_spmd.clone.clone.sunk | while | flops 87085088 | bytes 3328036 | solution.py:170
  35.4 5.8 %all_gather.29 = f32[16,2048]{1,0:T(8,128)S(1)} all-gather(f32[16,512]{1,0:T(8,128)S(1)} %get-tuple-element.1379), channel_id=1, replica_groups=mesh['day'=8,'pt'=4] {'pt'}, dimensions={1}, use_global_device_ids=true | all-gather | bytes 163840 | tf_op jit(solution)/shard_map/while/body/eval_jaxpr/all_gather | solution.py:137
  57.4 5.7 %all_gather.29 = f32[16,2048]{1,0:T(8,128)S(1)} all-gather(f32[16,512]{1,0:T(8,128)S(1)} %get-tuple-element.1379), channel_id=1, replica_groups=mesh['day'=8,'pt'=4] {'pt'}, dimensions={1}, use_global_device_ids=true | all-gather | bytes 163840 | tf_op jit(solution)/shard_map/while/body/eval_jaxpr/all_gather | solution.py:137
  63.5 9.9 %collective-permute-start.3 = (bf16[16,2048]{1,0:T(8,128)(2,1)S(1)}, bf16[16,2048]{1,0:T(8,128)(2,1)S(1)}, u32[]{:S(2)}, u32[]{:S(2)}) collective-permute-start(bf16[16,2048]{1,0:T(8,128)(2,1)S(1)} %get-tuple-element.1384), channel_id=1, source_target_pairs={{0,4},{4,8},{8,12},{12,16},{16,20},{20,24},{24,28},{1,5},{5,9},{9,... | collective-permute-start | bytes 196616 | tf_op jit(solution)/shard_map/while/body/eval_jaxpr/ppermute | solution.py:40
  90.9 9.3 %collective-permute-start.3 = (bf16[16,2048]{1,0:T(8,128)(2,1)S(1)}, bf16[16,2048]{1,0:T(8,128)(2,1)S(1)}, u32[]{:S(2)}, u32[]{:S(2)}) collective-permute-start(bf16[16,2048]{1,0:T(8,128)(2,1)S(1)} %get-tuple-element.1384), channel_id=1, source_target_pairs={{0,4},{4,8},{8,12},{12,16},{16,20},{20,24},{24,28},{1,5},{5,9},{9,... | collective-permute-start | bytes 196616 | tf_op jit(solution)/shard_map/while/body/eval_jaxpr/ppermute | solution.py:40
  117.7 9.3 %collective-permute-start.3 = (bf16[16,2048]{1,0:T(8,128)(2,1)S(1)}, bf16[16,2048]{1,0:T(8,128)(2,1)S(1)}, u32[]{:S(2)}, u32[]{:S(2)}) collective-permute-start(bf16[16,2048]{1,0:T(8,128)(2,1)S(1)} %get-tuple-element.1384), channel_id=1, source_target_pairs={{0,4},{4,8},{8,12},{12,16},{16,20},{20,24},{24,28},{1,5},{5,9},{9,... | collective-permute-start | bytes 196616 | tf_op jit(solution)/shard_map/while/body/eval_jaxpr/ppermute | solution.py:40
  144.5 9.3 %collective-permute-start.3 = (bf16[16,2048]{1,0:T(8,128)(2,1)S(1)}, bf16[16,2048]{1,0:T(8,128)(2,1)S(1)}, u32[]{:S(2)}, u32[]{:S(2)}) collective-permute-start(bf16[16,2048]{1,0:T(8,128)(2,1)S(1)} %get-tuple-element.1384), channel_id=1, source_target_pairs={{0,4},{4,8},{8,12},{12,16},{16,20},{20,24},{24,28},{1,5},{5,9},{9,... | collective-permute-start | bytes 196616 | tf_op jit(solution)/shard_map/while/body/eval_jaxpr/ppermute | solution.py:40
  171.3 11.0 %collective-permute-start.3 = (bf16[16,2048]{1,0:T(8,128)(2,1)S(1)}, bf16[16,2048]{1,0:T(8,128)(2,1)S(1)}, u32[]{:S(2)}, u32[]{:S(2)}) collective-permute-start(bf16[16,2048]{1,0:T(8,128)(2,1)S(1)} %get-tuple-element.1384), channel_id=1, source_target_pairs={{0,4},{4,8},{8,12},{12,16},{16,20},{20,24},{24,28},{1,5},{5,9},{9,... | collective-permute-start | bytes 196616 | tf_op jit(solution)/shard_map/while/body/eval_jaxpr/ppermute | solution.py:40
  184.2 17.1 %collective-permute-done.4 = bf16[16,2048]{1,0:T(8,128)(2,1)S(1)} collective-permute-done((bf16[16,2048]{1,0:T(8,128)(2,1)S(1)}, bf16[16,2048]{1,0:T(8,128)(2,1)S(1)}, u32[]{:S(2)}, u32[]{:S(2)}) %collective-permute-start.4) | collective-permute-done | bytes 65568 | tf_op jit(solution)/shard_map/while/body/eval_jaxpr/ppermute | solution.py:40
  212.7 11.2 %collective-permute-start.3 = (bf16[16,2048]{1,0:T(8,128)(2,1)S(1)}, bf16[16,2048]{1,0:T(8,128)(2,1)S(1)}, u32[]{:S(2)}, u32[]{:S(2)}) collective-permute-start(bf16[16,2048]{1,0:T(8,128)(2,1)S(1)} %get-tuple-element.1384), channel_id=1, source_target_pairs={{0,4},{4,8},{8,12},{12,16},{16,20},{20,24},{24,28},{1,5},{5,9},{9,... | collective-permute-start | bytes 196616 | tf_op jit(solution)/shard_map/while/body/eval_jaxpr/ppermute | solution.py:40
  230.1 7.0 %conditional.8 = (f32[16,512]{1,0:T(8,128)}) conditional(s32[]{:T(128)} %convert_element_type.141, () %tuple.161, (bf16[16,2048]{1,0:T(8,128)(2,1)S(1)}, f32[2048]{0:T(1024)S(1)}, f32[512]{0:T(512)S(1)}, bf16[64,2048]{1,0:T(8,128)(2,1)S(1)}, bf16[64,512]{1,0:T(8,128)(2,1)S(1)}) %tuple.162), branch_computations={%region_9.9_spmd, %region_10.12_spmd} | conditional | flops 43270152 | bytes 222992 | solution.py:130
  230.1 7.0 %while.70 = (s32[]{:T(128)}, f32[16,512]{1,0:T(8,128)}, bf16[16,2048]{1,0:T(8,128)(2,1)S(1)}, f32[2048]{0:T(1024)S(1)}, f32[512]{0:T(512)S(1)}, /*index=5*/bf16[...) while((s32[]{:T(128)}, f32[16,512]{1,0:T(8,128)}, ...), condition=%wide.region_12.11_spmd.clone, body=%wide.region_11.10_spmd.clone.sunk | while | flops 43270152 | bytes 222888 | solution.py:99
  247.8 7.5 %collective-permute-start.3 = (bf16[16,2048]{1,0:T(8,128)(2,1)S(1)}, bf16[16,2048]{1,0:T(8,128)(2,1)S(1)}, u32[]{:S(2)}, u32[]{:S(2)}) collective-permute-start(bf16[16,2048]{1,0:T(8,128)(2,1)S(1)} %get-tuple-element.1384), channel_id=1, source_target_pairs={{0,4},{4,8},{8,12},{12,16},{16,20},{20,24},{24,28},{1,5},{5,9},{9,... | collective-permute-start | bytes 196616 | tf_op jit(solution)/shard_map/while/body/eval_jaxpr/ppermute | solution.py:40
  261.4 7.1 %conditional.8 = (f32[16,512]{1,0:T(8,128)}) conditional(s32[]{:T(128)} %convert_element_type.141, () %tuple.161, (bf16[16,2048]{1,0:T(8,128)(2,1)S(1)}, f32[2048]{0:T(1024)S(1)}, f32[512]{0:T(512)S(1)}, bf16[64,2048]{1,0:T(8,128)(2,1)S(1)}, bf16[64,512]{1,0:T(8,128)(2,1)S(1)}) %tuple.162), branch_computations={%region_9.9_spmd, %region_10.12_spmd} | conditional | flops 43270152 | bytes 222992 | solution.py:130
  261.5 7.0 %while.70 = (s32[]{:T(128)}, f32[16,512]{1,0:T(8,128)}, bf16[16,2048]{1,0:T(8,128)(2,1)S(1)}, f32[2048]{0:T(1024)S(1)}, f32[512]{0:T(512)S(1)}, /*index=5*/bf16[...) while((s32[]{:T(128)}, f32[16,512]{1,0:T(8,128)}, ...), condition=%wide.region_12.11_spmd.clone, body=%wide.region_11.10_spmd.clone.sunk | while | flops 43270152 | bytes 222888 | solution.py:99
  290.2 7.1 %conditional.8 = (f32[16,512]{1,0:T(8,128)}) conditional(s32[]{:T(128)} %convert_element_type.141, () %tuple.161, (bf16[16,2048]{1,0:T(8,128)(2,1)S(1)}, f32[2048]{0:T(1024)S(1)}, f32[512]{0:T(512)S(1)}, bf16[64,2048]{1,0:T(8,128)(2,1)S(1)}, bf16[64,512]{1,0:T(8,128)(2,1)S(1)}) %tuple.162), branch_computations={%region_9.9_spmd, %region_10.12_spmd} | conditional | flops 43270152 | bytes 222992 | solution.py:130
  290.2 7.1 %while.70 = (s32[]{:T(128)}, f32[16,512]{1,0:T(8,128)}, bf16[16,2048]{1,0:T(8,128)(2,1)S(1)}, f32[2048]{0:T(1024)S(1)}, f32[512]{0:T(512)S(1)}, /*index=5*/bf16[...) while((s32[]{:T(128)}, f32[16,512]{1,0:T(8,128)}, ...), condition=%wide.region_12.11_spmd.clone, body=%wide.region_11.10_spmd.clone.sunk | while | flops 43270152 | bytes 222888 | solution.py:99
  317.0 7.0 %conditional.8 = (f32[16,512]{1,0:T(8,128)}) conditional(s32[]{:T(128)} %convert_element_type.141, () %tuple.161, (bf16[16,2048]{1,0:T(8,128)(2,1)S(1)}, f32[2048]{0:T(1024)S(1)}, f32[512]{0:T(512)S(1)}, bf16[64,2048]{1,0:T(8,128)(2,1)S(1)}, bf16[64,512]{1,0:T(8,128)(2,1)S(1)}) %tuple.162), branch_computations={%region_9.9_spmd, %region_10.12_spmd} | conditional | flops 43270152 | bytes 222992 | solution.py:130
  317.0 7.0 %while.70 = (s32[]{:T(128)}, f32[16,512]{1,0:T(8,128)}, bf16[16,2048]{1,0:T(8,128)(2,1)S(1)}, f32[2048]{0:T(1024)S(1)}, f32[512]{0:T(512)S(1)}, /*index=5*/bf16[...) while((s32[]{:T(128)}, f32[16,512]{1,0:T(8,128)}, ...), condition=%wide.region_12.11_spmd.clone, body=%wide.region_11.10_spmd.clone.sunk | while | flops 43270152 | bytes 222888 | solution.py:99
  347.5 25.9 %while.71 = (s32[]{:T(128)}, f32[8,2048]{1,0:T(8,128)S(1)}, s32[8]{0:T(128)S(1)}, f32[2048]{0:T(1024)S(1)}, f32[2048]{0:T(1024)S(1)}, /*index=5*/f32[2048]{0:T(1...) while((s32[]{:T(128)}, f32[8,2048]{1,0:T(8,128)S(1)}, ...), condition=%wide.region_20.21_spmd, body=%wide.region_19.20_spmd.sunk | while | flops 75497480 | bytes 4528319 | solution.py:198
  374.7 29.2 %while.72 = (s32[]{:T(128)}, f32[8,256]{1,0:T(8,128)S(1)}, s32[8]{0:T(128)S(1)}, f32[2048]{0:T(1024)S(1)}, f32[2048]{0:T(1024)S(1)}, /*index=5*/bf16[64,2048]{1,...) while((s32[]{:T(128)}, f32[8,256]{1,0:T(8,128)S(1)}, ...), condition=%wide.region_23.24_spmd, body=%wide.region_22.23_spmd.sunk | while | flops 75497480 | bytes 4511931 | solution.py:207
  403.9 7.2 %all-reduce = f32[2048]{0:T(1024)S(1)} all-reduce(f32[2048]{0:T(1024)S(1)} %bitcast.86), channel_id=2, replica_groups=mesh['day'=8,'pt'=4] {'pt'}, use_global_device_ids=true, to_apply=%region_24.25.clone | all-reduce | flops 2048 | bytes 16384
  (468 shorter events, 288.9 us)
Async XLA Ops:
  8.3 21.4 %collective-permute-start.6 = (bf16[1,64,2048]{2,1,0:T(8,128)(2,1)S(1)}, bf16[1,64,2048]{2,1,0:T(8,128)(2,1)S(1)}, u32[]{:S(2)}, u32[]{:S(2)}) collective-permute-start(bf16[1,64,2048]{2,1,0:T(8,128)(2,1)S(1)} %all_gather.22), channel_id=1, source_target_pairs={{4,0},{8,4},{12,8},{16,12},{20,16},{24,20},{28,24},{5,1},{9,5},{13... | collective-permute-start | bytes 786440 | tf_op jit(solution)/shard_map/ppermute | solution.py:30
  9.5 20.2 %collective-permute-start.5 = (bf16[1,64,2048]{2,1,0:T(8,128)(2,1)S(1)}, bf16[1,64,2048]{2,1,0:T(8,128)(2,1)S(1)}, u32[]{:S(2)}, u32[]{:S(2)}) collective-permute-start(bf16[1,64,2048]{2,1,0:T(8,128)(2,1)S(1)} %all_gather.22), channel_id=1, source_target_pairs={{0,4},{4,8},{8,12},{12,16},{16,20},{20,24},{24,28},{1,5},{5,9},{9,... | collective-permute-start | bytes 786440 | tf_op jit(solution)/shard_map/ppermute | solution.py:28
  32.4 8.8 %collective-permute-start.2 = (f32[16,512]{1,0:T(8,128)S(1)}, f32[16,512]{1,0:T(8,128)S(1)}, u32[]{:S(2)}, u32[]{:S(2)}) collective-permute-start(f32[16,512]{1,0:T(8,128)S(1)} %get-tuple-element.1378), channel_id=1, source_target_pairs={{0,3},{1,0},{2,1},{3,2},{4,7},{5,4},{6,5},{7,6},{8,11},{9,8},{10,9... | collective-permute-start | bytes 98312 | tf_op jit(solution)/shard_map/while/body/eval_jaxpr/ppermute | solution.py:15
  41.5 6.2 %collective-permute-start.3 = (bf16[16,2048]{1,0:T(8,128)(2,1)S(1)}, bf16[16,2048]{1,0:T(8,128)(2,1)S(1)}, u32[]{:S(2)}, u32[]{:S(2)}) collective-permute-start(bf16[16,2048]{1,0:T(8,128)(2,1)S(1)} %get-tuple-element.1384), channel_id=1, source_target_pairs={{0,4},{4,8},{8,12},{12,16},{16,20},{20,24},{24,28},{1,5},{5,9},{9,... | collective-permute-start | bytes 196616 | tf_op jit(solution)/shard_map/while/body/eval_jaxpr/ppermute | solution.py:40
  54.1 9.1 %collective-permute-start.2 = (f32[16,512]{1,0:T(8,128)S(1)}, f32[16,512]{1,0:T(8,128)S(1)}, u32[]{:S(2)}, u32[]{:S(2)}) collective-permute-start(f32[16,512]{1,0:T(8,128)S(1)} %get-tuple-element.1378), channel_id=1, source_target_pairs={{0,3},{1,0},{2,1},{3,2},{4,7},{5,4},{6,5},{7,6},{8,11},{9,8},{10,9... | collective-permute-start | bytes 98312 | tf_op jit(solution)/shard_map/while/body/eval_jaxpr/ppermute | solution.py:15
  63.5 11.8 %collective-permute-start.3 = (bf16[16,2048]{1,0:T(8,128)(2,1)S(1)}, bf16[16,2048]{1,0:T(8,128)(2,1)S(1)}, u32[]{:S(2)}, u32[]{:S(2)}) collective-permute-start(bf16[16,2048]{1,0:T(8,128)(2,1)S(1)} %get-tuple-element.1384), channel_id=1, source_target_pairs={{0,4},{4,8},{8,12},{12,16},{16,20},{20,24},{24,28},{1,5},{5,9},{9,... | collective-permute-start | bytes 196616 | tf_op jit(solution)/shard_map/while/body/eval_jaxpr/ppermute | solution.py:40
  81.6 8.9 %collective-permute-start.2 = (f32[16,512]{1,0:T(8,128)S(1)}, f32[16,512]{1,0:T(8,128)S(1)}, u32[]{:S(2)}, u32[]{:S(2)}) collective-permute-start(f32[16,512]{1,0:T(8,128)S(1)} %get-tuple-element.1378), channel_id=1, source_target_pairs={{0,3},{1,0},{2,1},{3,2},{4,7},{5,4},{6,5},{7,6},{8,11},{9,8},{10,9... | collective-permute-start | bytes 98312 | tf_op jit(solution)/shard_map/while/body/eval_jaxpr/ppermute | solution.py:15
  90.9 11.2 %collective-permute-start.3 = (bf16[16,2048]{1,0:T(8,128)(2,1)S(1)}, bf16[16,2048]{1,0:T(8,128)(2,1)S(1)}, u32[]{:S(2)}, u32[]{:S(2)}) collective-permute-start(bf16[16,2048]{1,0:T(8,128)(2,1)S(1)} %get-tuple-element.1384), channel_id=1, source_target_pairs={{0,4},{4,8},{8,12},{12,16},{16,20},{20,24},{24,28},{1,5},{5,9},{9,... | collective-permute-start | bytes 196616 | tf_op jit(solution)/shard_map/while/body/eval_jaxpr/ppermute | solution.py:40
  108.5 8.9 %collective-permute-start.2 = (f32[16,512]{1,0:T(8,128)S(1)}, f32[16,512]{1,0:T(8,128)S(1)}, u32[]{:S(2)}, u32[]{:S(2)}) collective-permute-start(f32[16,512]{1,0:T(8,128)S(1)} %get-tuple-element.1378), channel_id=1, source_target_pairs={{0,3},{1,0},{2,1},{3,2},{4,7},{5,4},{6,5},{7,6},{8,11},{9,8},{10,9... | collective-permute-start | bytes 98312 | tf_op jit(solution)/shard_map/while/body/eval_jaxpr/ppermute | solution.py:15
  117.7 11.2 %collective-permute-start.3 = (bf16[16,2048]{1,0:T(8,128)(2,1)S(1)}, bf16[16,2048]{1,0:T(8,128)(2,1)S(1)}, u32[]{:S(2)}, u32[]{:S(2)}) collective-permute-start(bf16[16,2048]{1,0:T(8,128)(2,1)S(1)} %get-tuple-element.1384), channel_id=1, source_target_pairs={{0,4},{4,8},{8,12},{12,16},{16,20},{20,24},{24,28},{1,5},{5,9},{9,... | collective-permute-start | bytes 196616 | tf_op jit(solution)/shard_map/while/body/eval_jaxpr/ppermute | solution.py:40
  135.3 8.9 %collective-permute-start.2 = (f32[16,512]{1,0:T(8,128)S(1)}, f32[16,512]{1,0:T(8,128)S(1)}, u32[]{:S(2)}, u32[]{:S(2)}) collective-permute-start(f32[16,512]{1,0:T(8,128)S(1)} %get-tuple-element.1378), channel_id=1, source_target_pairs={{0,3},{1,0},{2,1},{3,2},{4,7},{5,4},{6,5},{7,6},{8,11},{9,8},{10,9... | collective-permute-start | bytes 98312 | tf_op jit(solution)/shard_map/while/body/eval_jaxpr/ppermute | solution.py:15
  144.5 11.2 %collective-permute-start.3 = (bf16[16,2048]{1,0:T(8,128)(2,1)S(1)}, bf16[16,2048]{1,0:T(8,128)(2,1)S(1)}, u32[]{:S(2)}, u32[]{:S(2)}) collective-permute-start(bf16[16,2048]{1,0:T(8,128)(2,1)S(1)} %get-tuple-element.1384), channel_id=1, source_target_pairs={{0,4},{4,8},{8,12},{12,16},{16,20},{20,24},{24,28},{1,5},{5,9},{9,... | collective-permute-start | bytes 196616 | tf_op jit(solution)/shard_map/while/body/eval_jaxpr/ppermute | solution.py:40
  162.1 8.9 %collective-permute-start.2 = (f32[16,512]{1,0:T(8,128)S(1)}, f32[16,512]{1,0:T(8,128)S(1)}, u32[]{:S(2)}, u32[]{:S(2)}) collective-permute-start(f32[16,512]{1,0:T(8,128)S(1)} %get-tuple-element.1378), channel_id=1, source_target_pairs={{0,3},{1,0},{2,1},{3,2},{4,7},{5,4},{6,5},{7,6},{8,11},{9,8},{10,9... | collective-permute-start | bytes 98312 | tf_op jit(solution)/shard_map/while/body/eval_jaxpr/ppermute | solution.py:15
  171.3 12.9 %collective-permute-start.3 = (bf16[16,2048]{1,0:T(8,128)(2,1)S(1)}, bf16[16,2048]{1,0:T(8,128)(2,1)S(1)}, u32[]{:S(2)}, u32[]{:S(2)}) collective-permute-start(bf16[16,2048]{1,0:T(8,128)(2,1)S(1)} %get-tuple-element.1384), channel_id=1, source_target_pairs={{0,4},{4,8},{8,12},{12,16},{16,20},{20,24},{24,28},{1,5},{5,9},{9,... | collective-permute-start | bytes 196616 | tf_op jit(solution)/shard_map/while/body/eval_jaxpr/ppermute | solution.py:40
  182.3 19.0 %collective-permute-start.4 = (bf16[16,2048]{1,0:T(8,128)(2,1)S(1)}, bf16[16,2048]{1,0:T(8,128)(2,1)S(1)}, u32[]{:S(2)}, u32[]{:S(2)}) collective-permute-start(bf16[16,2048]{1,0:T(8,128)(2,1)S(1)} %get-tuple-element.1385), channel_id=1, source_target_pairs={{4,0},{8,4},{12,8},{16,12},{20,16},{24,20},{28,24},{5,1},{9,5},{13... | collective-permute-start | bytes 196616 | tf_op jit(solution)/shard_map/while/body/eval_jaxpr/ppermute | solution.py:40
  203.4 9.0 %collective-permute-start.2 = (f32[16,512]{1,0:T(8,128)S(1)}, f32[16,512]{1,0:T(8,128)S(1)}, u32[]{:S(2)}, u32[]{:S(2)}) collective-permute-start(f32[16,512]{1,0:T(8,128)S(1)} %get-tuple-element.1378), channel_id=1, source_target_pairs={{0,3},{1,0},{2,1},{3,2},{4,7},{5,4},{6,5},{7,6},{8,11},{9,8},{10,9... | collective-permute-start | bytes 98312 | tf_op jit(solution)/shard_map/while/body/eval_jaxpr/ppermute | solution.py:15
  212.7 13.1 %collective-permute-start.3 = (bf16[16,2048]{1,0:T(8,128)(2,1)S(1)}, bf16[16,2048]{1,0:T(8,128)(2,1)S(1)}, u32[]{:S(2)}, u32[]{:S(2)}) collective-permute-start(bf16[16,2048]{1,0:T(8,128)(2,1)S(1)} %get-tuple-element.1384), channel_id=1, source_target_pairs={{0,4},{4,8},{8,12},{12,16},{16,20},{20,24},{24,28},{1,5},{5,9},{9,... | collective-permute-start | bytes 196616 | tf_op jit(solution)/shard_map/while/body/eval_jaxpr/ppermute | solution.py:40
  238.6 8.9 %collective-permute-start.2 = (f32[16,512]{1,0:T(8,128)S(1)}, f32[16,512]{1,0:T(8,128)S(1)}, u32[]{:S(2)}, u32[]{:S(2)}) collective-permute-start(f32[16,512]{1,0:T(8,128)S(1)} %get-tuple-element.1378), channel_id=1, source_target_pairs={{0,3},{1,0},{2,1},{3,2},{4,7},{5,4},{6,5},{7,6},{8,11},{9,8},{10,9... | collective-permute-start | bytes 98312 | tf_op jit(solution)/shard_map/while/body/eval_jaxpr/ppermute | solution.py:15
  247.8 9.4 %collective-permute-start.3 = (bf16[16,2048]{1,0:T(8,128)(2,1)S(1)}, bf16[16,2048]{1,0:T(8,128)(2,1)S(1)}, u32[]{:S(2)}, u32[]{:S(2)}) collective-permute-start(bf16[16,2048]{1,0:T(8,128)(2,1)S(1)} %get-tuple-element.1384), channel_id=1, source_target_pairs={{0,4},{4,8},{8,12},{12,16},{16,20},{20,24},{24,28},{1,5},{5,9},{9,... | collective-permute-start | bytes 196616 | tf_op jit(solution)/shard_map/while/body/eval_jaxpr/ppermute | solution.py:40
  269.9 9.0 %collective-permute-start.2 = (f32[16,512]{1,0:T(8,128)S(1)}, f32[16,512]{1,0:T(8,128)S(1)}, u32[]{:S(2)}, u32[]{:S(2)}) collective-permute-start(f32[16,512]{1,0:T(8,128)S(1)} %get-tuple-element.1378), channel_id=1, source_target_pairs={{0,3},{1,0},{2,1},{3,2},{4,7},{5,4},{6,5},{7,6},{8,11},{9,8},{10,9... | collective-permute-start | bytes 98312 | tf_op jit(solution)/shard_map/while/body/eval_jaxpr/ppermute | solution.py:15
  279.2 6.6 %collective-permute-start.3 = (bf16[16,2048]{1,0:T(8,128)(2,1)S(1)}, bf16[16,2048]{1,0:T(8,128)(2,1)S(1)}, u32[]{:S(2)}, u32[]{:S(2)}) collective-permute-start(bf16[16,2048]{1,0:T(8,128)(2,1)S(1)} %get-tuple-element.1384), channel_id=1, source_target_pairs={{0,4},{4,8},{8,12},{12,16},{16,20},{20,24},{24,28},{1,5},{5,9},{9,... | collective-permute-start | bytes 196616 | tf_op jit(solution)/shard_map/while/body/eval_jaxpr/ppermute | solution.py:40
  298.7 8.9 %collective-permute-start.2 = (f32[16,512]{1,0:T(8,128)S(1)}, f32[16,512]{1,0:T(8,128)S(1)}, u32[]{:S(2)}, u32[]{:S(2)}) collective-permute-start(f32[16,512]{1,0:T(8,128)S(1)} %get-tuple-element.1378), channel_id=1, source_target_pairs={{0,3},{1,0},{2,1},{3,2},{4,7},{5,4},{6,5},{7,6},{8,11},{9,8},{10,9... | collective-permute-start | bytes 98312 | tf_op jit(solution)/shard_map/while/body/eval_jaxpr/ppermute | solution.py:15
  325.4 8.9 %collective-permute-start.2 = (f32[16,512]{1,0:T(8,128)S(1)}, f32[16,512]{1,0:T(8,128)S(1)}, u32[]{:S(2)}, u32[]{:S(2)}) collective-permute-start(f32[16,512]{1,0:T(8,128)S(1)} %get-tuple-element.1378), channel_id=1, source_target_pairs={{0,3},{1,0},{2,1},{3,2},{4,7},{5,4},{6,5},{7,6},{8,11},{9,8},{10,9... | collective-permute-start | bytes 98312 | tf_op jit(solution)/shard_map/while/body/eval_jaxpr/ppermute | solution.py:15
  336.0 6.2 %collective-permute-start.4 = (bf16[16,2048]{1,0:T(8,128)(2,1)S(1)}, bf16[16,2048]{1,0:T(8,128)(2,1)S(1)}, u32[]{:S(2)}, u32[]{:S(2)}) collective-permute-start(bf16[16,2048]{1,0:T(8,128)(2,1)S(1)} %get-tuple-element.1385), channel_id=1, source_target_pairs={{4,0},{8,4},{12,8},{16,12},{20,16},{24,20},{28,24},{5,1},{9,5},{13... | collective-permute-start | bytes 196616 | tf_op jit(solution)/shard_map/while/body/eval_jaxpr/ppermute | solution.py:40
  (40 other events, 880.5 us)
